TPU v7x, 32 devices: a whole 2x2x4 slice. The times are simulated.
32 devices in a mesh: dp: 8 (over z, y), region: 4 (over x, core).
Axes of the slice: x: 2, y: 2, z: 4, core: 2. Of those that a mesh axis runs over, the one named last changes fastest.
Arguments:
- travel_times: float32 [512, 128], P('dp'), may hold values from -60 to 60
- sensitivity: bfloat16 [512, 8, 128, 128], P('dp', 'region'), may hold values from -0.1875 to 0.1875
- tile_blocks: int32 [512, 8], P('dp', 'region'), may hold values from 0 to 1023
- face_blocks: int32 [1024, 2], P(('dp', 'region')), may hold values from 0 to 1023, as said below
- face_weights: float32 [1024, 128], P(('dp', 'region')), may hold values from 0.2 to 2
- face_count: int32 [32], P(('dp', 'region')), may hold values from 8 to 32, as said below
Outputs:
- solution: float32 [1024, 128], P('region')
Inputs may be any that keep to these rules, and one draw needn't show every extreme that they name: `face_blocks`: the first block of a face lies in the region of the device that holds the face, the second in that region or in the region one step up or down, the regions closing into a loop. `face_count`: entry k counts the faces in use among the 32 rows held by device k of dp+region; they are its first rows; some device holds 32.
All inputs are finite; a program needn't handle non-finite values.
Results may differ from a plain program's by a relative error of at most 0.0025.
The roundings to bfloat16 on the way count: a program that leaves them out, or rounds other values in their place, can miss the bound.
Values may be sent and summed in bfloat16 or wider, within the bound.
No kernel may reach another device: no remote copies, remote signals or barrier semaphores. Data moves between devices by JAX's collectives and lax.ppermute only.
A program may use at most 64 MiB of HBM per device.

v0:
```python
import jax
import jax.numpy as jnp
from jax import lax
from jax.sharding import PartitionSpec as P

ITERS = 2
NB_DEV = 256
smooth_weight = 1.0


def reduce_partials(partials):
    summed = lax.psum(partials, ("dp", "region"))
    return lax.dynamic_slice_in_dim(summed, lax.axis_index("region") * NB_DEV, NB_DEV, 0)


def piece_squares(piece):
    local_sq = jnp.sum(piece * piece)
    return lax.psum(local_sq, "region")


def model_field(piece):
    slab_half = piece.astype(jnp.bfloat16)
    return lax.all_gather(slab_half, "region", axis=0, tiled=True)


def left_squares(ray_sq, face_sq):
    return lax.psum(ray_sq, "dp") + lax.psum(face_sq, ("dp", "region"))


def local(travel_times, sensitivity, tile_blocks, face_blocks, face_weights, face_count):
    model_rows = NB_DEV * lax.axis_size("region")
    live_mask = (jnp.arange(face_blocks.shape[0]) < face_count[0]).astype(jnp.float32)
    face_scale = smooth_weight * face_weights * live_mask[:, None]
    first_block = face_blocks[:, 0]
    second_block = face_blocks[:, 1]
    flat_blocks = tile_blocks.reshape(-1)

    def transposed(left_rays, left_faces):
        rays_half = left_rays.astype(jnp.bfloat16)
        contrib = jnp.einsum(
            "tsrb,tr->tsb", sensitivity, rays_half, preferred_element_type=jnp.float32
        )
        contrib_rows = contrib.reshape(-1, contrib.shape[-1])
        face_term = face_scale * left_faces
        partials = jax.ops.segment_sum(contrib_rows, flat_blocks, num_segments=model_rows)
        partials = partials + jax.ops.segment_sum(face_term, first_block, num_segments=model_rows)
        partials = partials - jax.ops.segment_sum(face_term, second_block, num_segments=model_rows)
        return reduce_partials(partials)

    beta_value = jnp.sqrt(
        left_squares(jnp.sum(travel_times * travel_times), jnp.zeros((), jnp.float32))
    )
    left_rays = travel_times / beta_value
    left_faces = jnp.zeros(face_weights.shape, jnp.float32)
    right_vector = transposed(left_rays, left_faces)
    alpha_value = jnp.sqrt(piece_squares(right_vector))
    right_vector = right_vector / alpha_value
    direction = right_vector
    solution = jnp.zeros_like(right_vector)
    phi_bar = beta_value
    rho_bar = alpha_value
    for iteration in range(ITERS):
        full_model = model_field(right_vector)
        picked = full_model[tile_blocks]
        partial_value = jnp.einsum(
            "tsrb,tsb->tr", sensitivity, picked, preferred_element_type=jnp.float32
        )
        ray_pred = lax.psum(partial_value.astype(jnp.bfloat16), "region").astype(jnp.float32)
        face_pred = face_scale * (
            full_model[first_block].astype(jnp.float32)
            - full_model[second_block].astype(jnp.float32)
        )
        ray_pred, face_pred = (ray_pred, face_pred)
        left_rays = ray_pred - alpha_value * left_rays
        left_faces = face_pred - alpha_value * left_faces
        beta_value = jnp.sqrt(
            left_squares(jnp.sum(left_rays * left_rays), jnp.sum(left_faces * left_faces))
        )
        left_rays = left_rays / beta_value
        left_faces = left_faces / beta_value
        last_turn = iteration + 1 == ITERS
        if not last_turn:
            right_vector = transposed(left_rays, left_faces) - beta_value * right_vector
            alpha_new = jnp.sqrt(piece_squares(right_vector))
            right_vector = right_vector / alpha_new
        rho_value = jnp.sqrt(rho_bar * rho_bar + beta_value * beta_value)
        cosine = rho_bar / rho_value
        sine_value = beta_value / rho_value
        phi_value = cosine * phi_bar
        phi_bar = sine_value * phi_bar
        solution = solution + phi_value / rho_value * direction
        if not last_turn:
            rho_bar = -cosine * alpha_new
            direction = right_vector - sine_value * alpha_new / rho_value * direction
            alpha_value = alpha_new
    return solution


def solution(mesh):
    in_specs = (
        P("dp", None),
        P("dp", "region", None, None),
        P("dp", "region"),
        P(("dp", "region"), None),
        P(("dp", "region"), None),
        P(("dp", "region")),
    )
    out_specs = P("region", None)
    return jax.shard_map(local, mesh=mesh, in_specs=in_specs, out_specs=out_specs, check_vma=False)
```

profile of v0, /device:TPU:12, one launch (start us, length us, event | category | flops | bytes accessed | tf_op | source)
XLA Modules:
  0.0 539.1 jit_solution(2553015749312402894)
XLA Ops:
  6.5 0.8 fusion.24
  7.3 0.8 copy.9
  8.7 1.4 multiply_reduce_fusion.4
  10.1 0.1 broadcast_in_dim_reshape.4
  10.2 15.8 %psum.84 = f32[]{:T(128)} all-reduce(f32[]{:T(128)} %multiply_reduce_fusion.4), channel_id=1, replica_groups=mesh['dp'=8,'region'=4] {'dp'}, use_global_device_ids=true, to_apply=%region_1.0 | all-reduce | flops 1 | bytes 8 | tf_op jit(solution)/shard_map/psum | solution.py:27
  26.0 46.4 %psum.85 = f32[]{:T(128)} all-reduce(f32[]{:T(128)} %constant.5.clone.1), channel_id=1, replica_groups=mesh['dp'=8,'region'=4] {'dp','region'}, use_global_device_ids=true, to_apply=%region_2.0 | all-reduce | flops 1 | bytes 8 | tf_op jit(solution)/shard_map/psum | solution.py:27
  73.8 0.8 convert_bitcast_fusion.1
  74.6 0.8 multiply_multiply_fusion.1
  75.4 1.1 scatter_custom_fusion.1
  76.5 2.8 fusion.21
  79.3 1.3 scatter_custom_fusion
  80.6 0.9 sub.30
  81.6 0.1 copy.10
  81.7 0.1 reshape.15
  81.8 126.7 %all-reduce.3.cloned.1.call-done = f32[1024,128]{1,0:T(8,128)} async-done(((f32[1024,128]{1,0:T(8,128)}), f32[1024,128]{1,0:T(8,128)}) %all-reduce.3.cloned.1.call-update) | async-done | bytes 524304 | tf_op jit(solution)/shard_map/psum | solution.py:12
  208.6 1.5 multiply_reduce_fusion.1
  210.1 6.3 %psum.87 = f32[]{:T(128)} all-reduce(f32[]{:T(128)} %multiply_reduce_fusion.1), channel_id=1, replica_groups=mesh['dp'=8,'region'=4] {'region'}, use_global_device_ids=true, to_apply=%region_7.0 | all-reduce | flops 1 | bytes 8 | tf_op jit(solution)/shard_map/psum | solution.py:18
  217.1 0.9 fusion.26
  218.0 5.8 %all_gather.6 = bf16[1024,128]{1,0:T(8,128)(2,1)S(1)} all-gather(bf16[256,128]{1,0:T(8,128)(2,1)S(1)} %fusion.26), channel_id=1, replica_groups=mesh['dp'=8,'region'=4] {'region'}, dimensions={0}, use_global_device_ids=true | all-gather | bytes 327680 | tf_op jit(solution)/shard_map/all_gather | solution.py:23
  223.8 0.7 gather_fusion
  224.5 3.4 fusion.16
  227.9 10.7 %psum.88 = bf16[64,128]{1,0:T(8,128)(2,1)S(1)} all-reduce(bf16[64,128]{1,0:T(8,128)(2,1)S(1)} %convert_element_type.46), channel_id=1, replica_groups=mesh['dp'=8,'region'=4] {'region'}, use_global_device_ids=true, to_apply=%region_8.0 | all-reduce | flops 8192 | bytes 32768 | tf_op jit(solution)/shard_map/psum | solution.py:68
  238.6 0.6 multiply_reduce_fusion.3
  239.2 0.6 gather_fusion.2
  239.8 0.6 gather_fusion.1
  240.4 0.8 multiply_reduce_fusion.6
  241.2 16.7 %psum.89 = f32[]{:T(128)} all-reduce(f32[]{:T(128)} %multiply_reduce_fusion.3), channel_id=1, replica_groups=mesh['dp'=8,'region'=4] {'dp'}, use_global_device_ids=true, to_apply=%region_10.0 | all-reduce | flops 1 | bytes 8 | tf_op jit(solution)/shard_map/psum | solution.py:27
  257.9 43.8 %psum.90 = f32[]{:T(128)} all-reduce(f32[]{:T(128)} %multiply_reduce_fusion.6), channel_id=1, replica_groups=mesh['dp'=8,'region'=4] {'dp','region'}, use_global_device_ids=true, to_apply=%region_12.0 | all-reduce | flops 1 | bytes 8 | tf_op jit(solution)/shard_map/psum | solution.py:27
  303.1 0.1 multiply_multiply_fusion
  303.2 2.8 fusion.19
  306.0 0.8 scatter_custom_fusion.3
  306.9 1.3 scatter_custom_fusion.2
  308.2 0.9 sub.34
  309.2 126.8 %all-reduce.5.cloned.1.call-done = f32[1024,128]{1,0:T(8,128)} async-done(((f32[1024,128]{1,0:T(8,128)}), f32[1024,128]{1,0:T(8,128)}) %all-reduce.5.cloned.1.call-update) | async-done | bytes 524304 | tf_op jit(solution)/shard_map/psum | solution.py:12
  436.0 1.6 multiply_reduce_fusion
  437.6 6.3 %psum.92 = f32[]{:T(128)} all-reduce(f32[]{:T(128)} %multiply_reduce_fusion), channel_id=1, replica_groups=mesh['dp'=8,'region'=4] {'region'}, use_global_device_ids=true, to_apply=%region_17.0 | all-reduce | flops 1 | bytes 8 | tf_op jit(solution)/shard_map/psum | solution.py:18
  444.6 0.9 fusion.18
  445.6 5.8 %all_gather.7 = bf16[1024,128]{1,0:T(8,128)(2,1)S(1)} all-gather(bf16[256,128]{1,0:T(8,128)(2,1)S(1)} %fusion.18), channel_id=1, replica_groups=mesh['dp'=8,'region'=4] {'region'}, dimensions={0}, use_global_device_ids=true | all-gather | bytes 327680 | tf_op jit(solution)/shard_map/all_gather | solution.py:23
  451.3 0.7 gather_fusion.3
  452.1 0.6 gather_fusion.5
  452.6 0.6 gather_fusion.4
  453.3 3.4 fusion.14
  456.7 10.6 %psum.93 = bf16[64,128]{1,0:T(8,128)(2,1)S(1)} all-reduce(bf16[64,128]{1,0:T(8,128)(2,1)S(1)} %convert_element_type.52), channel_id=1, replica_groups=mesh['dp'=8,'region'=4] {'region'}, use_global_device_ids=true, to_apply=%region_18.0 | all-reduce | flops 8192 | bytes 32768 | tf_op jit(solution)/shard_map/psum | solution.py:68
  467.3 0.6 multiply_reduce_fusion.2
  467.9 16.7 %psum.94 = f32[]{:T(128)} all-reduce(f32[]{:T(128)} %multiply_reduce_fusion.2), channel_id=1, replica_groups=mesh['dp'=8,'region'=4] {'dp'}, use_global_device_ids=true, to_apply=%region_20.0 | all-reduce | flops 1 | bytes 8 | tf_op jit(solution)/shard_map/psum | solution.py:27
  484.6 0.8 multiply_reduce_fusion.5
  485.4 43.8 %psum.95 = f32[]{:T(128)} all-reduce(f32[]{:T(128)} %multiply_reduce_fusion.5), channel_id=1, replica_groups=mesh['dp'=8,'region'=4] {'dp','region'}, use_global_device_ids=true, to_apply=%region_22.0 | all-reduce | flops 1 | bytes 8 | tf_op jit(solution)/shard_map/psum | solution.py:27
  530.7 1.6 multiply_add_fusion
  (20 shorter events, 0.1 us)
Async XLA Ops:
  6.5 75.0 %copy-start.3 = (s32[64,2]{0,1:T(2,128)S(1)}, s32[64,2]{0,1:T(2,128)}, u32[]{:S(2)}) copy-start(s32[64,2]{0,1:T(2,128)} %param.8) | copy-start | bytes 1540
  6.5 202.0 %all-reduce.3.cloned.1.call-start = ((), (), s32[]{:S(2)}) async-start(), calls=%async_computation | async-start | bytes 1048576 | tf_op jit(solution)/shard_map/psum | solution.py:12
  79.3 159.3 %copy-start.1 = (f32[64,128]{1,0:T(8,128)S(1)}, f32[64,128]{1,0:T(8,128)}, u32[]{:S(2)}) copy-start(f32[64,128]{1,0:T(8,128)} %param.6) | copy-start | bytes 98308
  79.3 161.1 %copy-start.2 = (f32[32,128]{1,0:T(8,128)S(1)}, f32[32,128]{1,0:T(8,128)}, u32[]{:S(2)}) copy-start(f32[32,128]{1,0:T(8,128)} %param.10) | copy-start | bytes 49156
  81.5 354.5 %all-reduce.5.cloned.1.call-start = ((), (), s32[]{:S(2)}) async-start(), calls=%async_computation.1 | async-start | bytes 1048576 | tf_op jit(solution)/shard_map/psum | solution.py:12
  227.9 208.1 %copy-start = (f32[1024,128]{1,0:T(8,128)S(1)}, f32[1024,128]{1,0:T(8,128)}, u32[]{:S(2)}) copy-start(f32[1024,128]{1,0:T(8,128)} %all-reduce.3.cloned.1.call-done) | copy-start | bytes 1572868
Sparse Core Ops, SparseCore 0:
  81.6 126.9 all-reduce.2
  309.2 126.7 all-reduce.4
where the time goes:
time: 540 us; the launch traced here: 539 us
  waiting for transfers between devices  254 us (47%)
  blocking collectives  229 us (42%)
  between operations  20.1 us (4%)
  other arithmetic  19.3 us (4%)
  matrix products  12.4 us (2%)
    psum x2, waiting for transfers between devices, reduce_partials(): summed = lax.psum(partials, ('dp', 'region'))  254 us
    psum x6, blocking collectives, left_squares(): return lax.psum(ray_sq, 'dp') + lax.psum(face_sq, ('dp', 'region'))  183 us
    psum x2, blocking collectives, local(): lax.psum(partial_value.astype(jnp.bfloat16), 'region').astype(jnp.float32)  21.3 us
    psum x2, blocking collectives, piece_squares(): return lax.psum(local_sq, 'region')  12.6 us
    all_gather x2, blocking collectives, model_field(): return lax.all_gather(slab_half, 'region', axis=0, tiled=True)  11.6 us
  transfers between devices with their start and end apart: 2, of which 2 were waited for; matrix products, arithmetic and copies ran while one was open for 0% of the time, Pallas kernels for 0%

commit v1 on v0

--- a/solution.py
+++ b/solution.py
@@ -6,6 +6,18 @@
 ITERS = 2
 NB_DEV = 256
 smooth_weight = 1.0
+
+
+def gather_by_bits(shard, axis, dim):
+    ways, here, turn = (lax.axis_size(axis), lax.axis_index(axis), shard.shape[dim])
+    line, have = (shard, 1)
+    while have < ways:
+        line = jnp.concatenate(
+            [line, lax.ppermute(line, axis, [(d, (d - have) % ways) for d in range(ways)])],
+            axis=dim,
+        )
+        have = 2 * have
+    return jnp.roll(line, here * turn, axis=dim)
 
 
 def reduce_partials(partials):
@@ -20,7 +32,7 @@
 
 def model_field(piece):
     slab_half = piece.astype(jnp.bfloat16)
-    return lax.all_gather(slab_half, "region", axis=0, tiled=True)
+    return gather_by_bits(slab_half, "region", 0)
 
 
 def left_squares(ray_sq, face_sq):

time: 540 us -> 550 us (1.019)
  waiting for transfers between devices: 254 us -> 265 us
  blocking collectives: 229 us -> 219 us
    ppermute x0 -> x4, waiting for transfers between devices: none -> 12.3 us  [gather_by_bits(): lax.ppermute(line, axis, [(d, (d - have) % ways) for d in range(ways)])]
    all_gather x2 -> x0, blocking collectives: 11.6 us -> none  [model_field(): return lax.all_gather(slab_half, 'region', axis=0, tiled=True)]
  transfers between devices with their start and end apart: 2 -> 6, of which waited for: 2 -> 6; matrix products, arithmetic and copies ran while one was open for 0% -> 0% of each run, Pallas kernels for 0% -> 0%
where the time goes in v1:
time: 550 us; the launch traced here: 549 us
  waiting for transfers between devices  265 us (48%)
  blocking collectives  219 us (40%)
  other arithmetic  24 us (4%)
  between operations  20.1 us (4%)
  matrix products  12.4 us (2%)
    psum x2, waiting for transfers between devices, reduce_partials(): summed = lax.psum(partials, ('dp', 'region'))  253 us
    psum x6, blocking collectives, left_squares(): return lax.psum(ray_sq, 'dp') + lax.psum(face_sq, ('dp', 'region'))  183 us
    psum x2, blocking collectives, local(): lax.psum(partial_value.astype(jnp.bfloat16), 'region').astype(jnp.float32)  23 us
    psum x2, blocking collectives, piece_squares(): return lax.psum(local_sq, 'region')  12.5 us
    ppermute x4, waiting for transfers between devices, gather_by_bits(): lax.ppermute(line, axis, [(d, (d - have) % ways) for d in range(ways)])  12.3 us
  transfers between devices with their start and end apart: 6, of which 6 were waited for; matrix products, arithmetic and copies ran while one was open for 0% of the time, Pallas kernels for 0%

profile of v1, /device:TPU:12, one launch (start us, length us, event | category | flops | bytes accessed | tf_op | source)
XLA Modules:
  0.0 549.1 jit_solution(6149810120157195198)
XLA Ops:
  6.5 0.8 fusion.34
  7.3 0.8 copy.9
  8.7 1.4 multiply_reduce_fusion.4
  10.2 15.8 %psum.84 = f32[]{:T(128)} all-reduce(f32[]{:T(128)} %multiply_reduce_fusion.4), channel_id=1, replica_groups=mesh['dp'=8,'region'=4] {'dp'}, use_global_device_ids=true, to_apply=%region_1.0 | all-reduce | flops 1 | bytes 8 | tf_op jit(solution)/shard_map/psum | solution.py:39
  26.0 46.4 %psum.85 = f32[]{:T(128)} all-reduce(f32[]{:T(128)} %constant.13.clone.1), channel_id=1, replica_groups=mesh['dp'=8,'region'=4] {'dp','region'}, use_global_device_ids=true, to_apply=%region_2.0 | all-reduce | flops 1 | bytes 8 | tf_op jit(solution)/shard_map/psum | solution.py:39
  73.8 0.8 convert_bitcast_fusion.1
  74.6 0.8 multiply_multiply_fusion.1
  75.4 1.1 scatter_custom_fusion.1
  76.5 2.8 fusion.31
  79.3 1.3 scatter_custom_fusion
  80.6 0.9 sub.33
  81.5 127.0 %all-reduce.3.cloned.1.call-done = f32[1024,128]{1,0:T(8,128)} async-done(((f32[1024,128]{1,0:T(8,128)}), f32[1024,128]{1,0:T(8,128)}) %all-reduce.3.cloned.1.call-update) | async-done | bytes 524304 | tf_op jit(solution)/shard_map/psum | solution.py:24
  208.5 1.5 multiply_reduce_fusion.1
  210.1 6.3 %psum.87 = f32[]{:T(128)} all-reduce(f32[]{:T(128)} %multiply_reduce_fusion.1), channel_id=1, replica_groups=mesh['dp'=8,'region'=4] {'region'}, use_global_device_ids=true, to_apply=%region_7.0 | all-reduce | flops 1 | bytes 8 | tf_op jit(solution)/shard_map/psum | solution.py:30
  217.0 0.9 fusion.36
  218.4 1.7 collective-permute-done
  220.1 1.4 collective-permute-start.1
  221.5 4.5 collective-permute-done.1
  226.0 2.3 fusion.7
  228.4 0.7 gather_fusion
  229.1 3.4 fusion.26
  232.4 11.5 %psum.88 = bf16[64,128]{1,0:T(8,128)(2,1)S(1)} all-reduce(bf16[64,128]{1,0:T(8,128)(2,1)S(1)} %convert_element_type.46), channel_id=1, replica_groups=mesh['dp'=8,'region'=4] {'region'}, use_global_device_ids=true, to_apply=%region_8.10 | all-reduce | flops 8192 | bytes 32768 | tf_op jit(solution)/shard_map/psum | solution.py:80
  244.0 0.6 multiply_reduce_fusion.3
  245.2 0.6 gather_fusion.1
  245.8 0.8 multiply_reduce_fusion.6
  246.6 15.8 %psum.89 = f32[]{:T(128)} all-reduce(f32[]{:T(128)} %multiply_reduce_fusion.3), channel_id=1, replica_groups=mesh['dp'=8,'region'=4] {'dp'}, use_global_device_ids=true, to_apply=%region_10.12 | all-reduce | flops 1 | bytes 8 | tf_op jit(solution)/shard_map/psum | solution.py:39
  262.3 44.8 %psum.90 = f32[]{:T(128)} all-reduce(f32[]{:T(128)} %multiply_reduce_fusion.6), channel_id=1, replica_groups=mesh['dp'=8,'region'=4] {'dp','region'}, use_global_device_ids=true, to_apply=%region_12.14 | all-reduce | flops 1 | bytes 8 | tf_op jit(solution)/shard_map/psum | solution.py:39
  308.6 2.8 fusion.29
  311.4 0.8 scatter_custom_fusion.3
  312.3 1.3 scatter_custom_fusion.2
  313.5 0.9 sub.37
  314.4 126.1 %all-reduce.5.cloned.1.call-done = f32[1024,128]{1,0:T(8,128)} async-done(((f32[1024,128]{1,0:T(8,128)}), f32[1024,128]{1,0:T(8,128)}) %all-reduce.5.cloned.1.call-update) | async-done | bytes 524304 | tf_op jit(solution)/shard_map/psum | solution.py:24
  440.5 1.6 multiply_reduce_fusion
  442.1 6.3 %psum.92 = f32[]{:T(128)} all-reduce(f32[]{:T(128)} %multiply_reduce_fusion), channel_id=1, replica_groups=mesh['dp'=8,'region'=4] {'region'}, use_global_device_ids=true, to_apply=%region_17.19 | all-reduce | flops 1 | bytes 8 | tf_op jit(solution)/shard_map/psum | solution.py:30
  449.1 0.9 fusion.28
  450.4 1.9 collective-permute-done.2
  452.3 1.4 collective-permute-start.3
  453.9 4.3 collective-permute-done.3
  458.2 2.3 fusion.2
  460.6 0.7 gather_fusion.3
  461.3 0.6 gather_fusion.5
  462.5 3.4 fusion.24
  465.8 11.4 %psum.93 = bf16[64,128]{1,0:T(8,128)(2,1)S(1)} all-reduce(bf16[64,128]{1,0:T(8,128)(2,1)S(1)} %convert_element_type.52), channel_id=1, replica_groups=mesh['dp'=8,'region'=4] {'region'}, use_global_device_ids=true, to_apply=%region_18.20 | all-reduce | flops 8192 | bytes 32768 | tf_op jit(solution)/shard_map/psum | solution.py:80
  477.2 0.6 multiply_reduce_fusion.2
  477.9 0.8 multiply_reduce_fusion.5
  478.6 15.8 %psum.94 = f32[]{:T(128)} all-reduce(f32[]{:T(128)} %multiply_reduce_fusion.2), channel_id=1, replica_groups=mesh['dp'=8,'region'=4] {'dp'}, use_global_device_ids=true, to_apply=%region_20.22 | all-reduce | flops 1 | bytes 8 | tf_op jit(solution)/shard_map/psum | solution.py:39
  494.4 44.8 %psum.95 = f32[]{:T(128)} all-reduce(f32[]{:T(128)} %multiply_reduce_fusion.5), channel_id=1, replica_groups=mesh['dp'=8,'region'=4] {'dp','region'}, use_global_device_ids=true, to_apply=%region_22.24 | all-reduce | flops 1 | bytes 8 | tf_op jit(solution)/shard_map/psum | solution.py:39
  540.7 1.6 multiply_add_fusion
  (30 shorter events, 2.3 us)
Async XLA Ops:
  6.5 211.6 %copy-start.3 = (s32[64,2]{0,1:T(2,128)S(1)}, s32[64,2]{0,1:T(2,128)}, u32[]{:S(2)}) copy-start(s32[64,2]{0,1:T(2,128)} %param.10) | copy-start | bytes 1540
  6.5 202.0 %all-reduce.3.cloned.1.call-start = ((), (), s32[]{:S(2)}) async-start(), calls=%async_computation | async-start | bytes 1048576 | tf_op jit(solution)/shard_map/psum | solution.py:24
  79.3 164.7 %copy-start.1 = (f32[64,128]{1,0:T(8,128)S(1)}, f32[64,128]{1,0:T(8,128)}, u32[]{:S(2)}) copy-start(f32[64,128]{1,0:T(8,128)} %param.8) | copy-start | bytes 98308
  80.6 165.2 %copy-start.2 = (f32[32,128]{1,0:T(8,128)S(1)}, f32[32,128]{1,0:T(8,128)}, u32[]{:S(2)}) copy-start(f32[32,128]{1,0:T(8,128)} %param.12) | copy-start | bytes 49156
  81.5 359.1 %all-reduce.5.cloned.1.call-start = ((), (), s32[]{:S(2)}) async-start(), calls=%async_computation.1 | async-start | bytes 1048576 | tf_op jit(solution)/shard_map/psum | solution.py:24
  218.0 2.1 collective-permute-start
  220.1 5.9 %collective-permute-start.1 = (bf16[512,128]{1,0:T(8,128)(2,1)S(1)}, bf16[512,128]{1,0:T(8,128)(2,1)S(1)}, u32[]{:S(2)}, u32[]{:S(2)}) collective-permute-start(bf16[512,128]{1,0:T(8,128)(2,1)S(1)} %pad_maximum_fusion), channel_id=1, source_target_pairs={{0,2},{1,3},{2,0},{3,1},{4,6},{5,7},{6,4},{7,5},{8,10},{9,11},{10,... | collective-permute-start | bytes 393224 | tf_op jit(solution)/shard_map/ppermute | solution.py:16
  232.4 208.1 %copy-start = (f32[1024,128]{1,0:T(8,128)S(1)}, f32[1024,128]{1,0:T(8,128)}, u32[]{:S(2)}) copy-start(f32[1024,128]{1,0:T(8,128)} %all-reduce.3.cloned.1.call-done) | copy-start | bytes 1572868
  450.0 2.3 collective-permute-start.2
  452.3 5.9 %collective-permute-start.3 = (bf16[512,128]{1,0:T(8,128)(2,1)S(1)}, bf16[512,128]{1,0:T(8,128)(2,1)S(1)}, u32[]{:S(2)}, u32[]{:S(2)}) collective-permute-start(bf16[512,128]{1,0:T(8,128)(2,1)S(1)} %pad_maximum_fusion.1), channel_id=1, source_target_pairs={{0,2},{1,3},{2,0},{3,1},{4,6},{5,7},{6,4},{7,5},{8,10},{9,11},{10,... | collective-permute-start | bytes 393224 | tf_op jit(solution)/shard_map/ppermute | solution.py:16
Sparse Core Ops, SparseCore 0:
  81.6 126.9 all-reduce.2
  314.5 125.9 all-reduce.4
